TPU v7x, 768 devices: a whole 4x8x12 slice. The times are simulated.
768 devices in a mesh: rep: 96 (over y_lo, z, core), fsdp: 8 (over y_hi, x).
Axes of the slice: x: 4, y: 8 (y_hi: 2, y_lo: 4; y = y_hi * 4 + y_lo), z: 12, core: 2. Of those that a mesh axis runs over, the one named last changes fastest.
Arguments:
- tokens: bfloat16 [393216, 2048], P(('rep', 'fsdp')), may hold values from -6 to 6
- out_grad: bfloat16 [393216, 256], P(('rep', 'fsdp')), may hold values from -6 to 6
- gain: float32 [96, 128], P('rep'), may hold values from 0.3 to 3
- inner_weight: float32 [96, 2048, 256], P('rep', 'fsdp'), may hold values from -6 to 6
- outer_weight: float32 [96, 2048, 256], P('rep', 'fsdp'), may hold values from -6.3 to 6.3
- momentum: float32 [96, 2048, 256], P('rep', 'fsdp'), may hold values from -1.2 to 1.2
- adam_m: float32 [96, 2048, 256], P('rep', 'fsdp'), may hold values from -2 to 2
- adam_v: float32 [96, 2048, 256], P('rep', 'fsdp'), may hold values from 0.5 to 8
- gossip_offset: int32 [1], replicated, may hold values from 0 to 65535
Outputs:
- outer_new: float32 [96, 2048, 256], P('rep', 'fsdp')
- momentum_new: float32 [96, 2048, 256], P('rep', 'fsdp')
- adam_m_new: float32 [96, 2048, 256], P('rep', 'fsdp')
- adam_v_new: float32 [96, 2048, 256], P('rep', 'fsdp')
All inputs are finite; a program needn't handle non-finite values.
Results may differ from a plain program's by a relative error of at most 0.0038.
Values may be sent and summed in bfloat16 or wider, within the bound.
No kernel may reach another device: no remote copies, remote signals or barrier semaphores. Data moves between devices by JAX's collectives and lax.ppermute only.
A program may use at most 32 MiB of HBM per device.

v0:
```python
import jax
import jax.numpy as jnp
from jax import lax
from jax.sharding import PartitionSpec as P

HEAD = 128
ADAM_STEP = 100


def from_behind(block, axis, distance):
    devices = range(lax.axis_size(axis))
    route = [((i - distance) % len(devices), i) for i in devices]
    return lax.ppermute(block, axis, route)


def gossip(values, offset, count_rep):
    def branch(distance):
        return lambda held: from_behind(held, "rep", distance)

    branches = [branch(distance) for distance in range(1, count_rep)]
    return lax.switch(offset - 1, branches, values)


def local(
    tokens, out_grad, gain, inner_weight, outer_weight, momentum, adam_m, adam_v, gossip_offset
):
    count_rep = lax.axis_size("rep")
    offset = 1 + gossip_offset[0] % (count_rep - 1)
    count_tok = tokens.shape[0]
    inner = inner_weight[0]
    outer = outer_weight[0]
    w_bf = inner.astype(jnp.bfloat16)
    columns = tokens
    count_fsdp = lax.axis_size("fsdp")
    w_copies = jnp.broadcast_to(w_bf[None], (count_fsdp,) + w_bf.shape)
    w_full = lax.all_to_all(w_copies, "fsdp", 0, 0, tiled=True).reshape(-1, w_bf.shape[1])
    keys = jnp.dot(columns, w_full, preferred_element_type=jnp.float32)
    heads = keys.reshape(count_tok, -1, HEAD)
    scale = lax.rsqrt(jnp.mean(heads * heads, axis=-1, keepdims=True) + 1e-06)
    unit = heads * scale
    g_out = out_grad.astype(jnp.float32).reshape(heads.shape) * gain[0]
    inner_prod = jnp.mean(unit * g_out, axis=-1, keepdims=True)
    key_grad = (scale * (g_out - unit * inner_prod)).reshape(keys.shape).astype(jnp.bfloat16)
    columns = tokens
    grad_terms = lax.dot_general(
        columns, key_grad, (((0,), (0,)), ((), ())), preferred_element_type=jnp.float32
    )
    grad_terms = grad_terms.reshape((count_fsdp, -1) + grad_terms.shape[1:])
    grad_parts = lax.all_to_all(grad_terms.astype(jnp.bfloat16), "fsdp", 0, 0, tiled=True)
    grad = grad_parts.astype(jnp.float32).sum(axis=0)
    first_new = 0.9 * adam_m[0] + 0.1 * grad
    second_new = 0.95 * adam_v[0] + 0.05 * grad * grad
    fix_one = 1.0 - 0.9**ADAM_STEP
    fix_two = 1.0 - 0.95**ADAM_STEP
    update = first_new / fix_one / (jnp.sqrt(second_new / fix_two) + 1e-08) + 0.1 * inner
    inner_next = inner - 0.05 * update
    delta = outer - inner_next
    outer_hi = outer.astype(jnp.bfloat16)
    outer_lo = (outer - outer_hi.astype(jnp.float32)).astype(jnp.bfloat16)
    sent = jnp.stack([outer_hi, outer_lo, delta.astype(jnp.bfloat16)])
    far = gossip(sent, offset, count_rep).astype(jnp.float32)
    outer_far = far[0] + far[1]
    delta_far = far[2]
    mean_delta = (delta + delta_far) / 2.0
    momentum_new = 0.9 * momentum[0] + mean_delta
    outer_new = (outer + outer_far) / 2.0 - 0.7 * (0.9 * momentum_new + mean_delta)
    return (outer_new[None], momentum_new[None], first_new[None], second_new[None])


def solution(mesh):
    return jax.shard_map(
        local,
        mesh=mesh,
        in_specs=(
            P(("rep", "fsdp"), None),
            P(("rep", "fsdp"), None),
            P("rep", None),
            P("rep", "fsdp", None),
            P("rep", "fsdp", None),
            P("rep", "fsdp", None),
            P("rep", "fsdp", None),
            P("rep", "fsdp", None),
            P(),
        ),
        out_specs=(
            P("rep", "fsdp", None),
            P("rep", "fsdp", None),
            P("rep", "fsdp", None),
            P("rep", "fsdp", None),
        ),
        check_vma=False,
    )
```

profile of v0, /device:TPU:65, one launch (start us, length us, event | category | flops | bytes accessed | tf_op | source)
XLA Modules:
  0.0 151.4 jit_solution(1527163686813690792)
XLA Ops:
  0.7 1.1 convert_bitcast_fusion
  1.9 1.1 broadcast_in_dim.5
  2.9 9.3 %all-to-all-start = ((bf16[8,256,256]{1,2,0:T(8,128)(2,1)}), bf16[8,256,256]{1,2,0:T(8,128)(2,1)}, u32[]{:S(2)}, u32[]{:S(2)}) async-start(bf16[8,256,256]{1,2,0:T(8,128)(2,1)} %broadcast_in_dim.5), calls=%async_computation | async-start | bytes 2097152 | tf_op jit(solution)/shard_map/all_to_all | solution.py:36
  12.4 20.5 %all-to-all-done = bf16[8,256,256]{1,2,0:T(8,128)(2,1)} async-done(((bf16[8,256,256]{1,2,0:T(8,128)(2,1)}), bf16[8,256,256]{1,2,0:T(8,128)(2,1)}, u32[]{:S(2)}, u32[]{:S(2)}) %all-to-all-start) | async-done | bytes 1048608 | tf_op jit(solution)/shard_map/all_to_all | solution.py:36
  32.9 2.2 %copy.132 = bf16[8,256,256]{2,1,0:T(8,128)(2,1)} copy(bf16[8,256,256]{1,2,0:T(8,128)(2,1)} %all-to-all-done) | data formatting | bytes 2097152 | tf_op jit(solution)/shard_map/all_to_all | solution.py:36
  35.2 2.3 %copy.133 = bf16[256,2048]{1,0:T(8,128)(2,1)} copy(bf16[256,2048]{0,1:T(8,128)(2,1)} %bitcast.33) | data formatting | bytes 2097152 | tf_op jit(solution)/shard_map/dot_general | solution.py:37
  37.4 2.0 %multiply_reduce_fusion.1 = (f32[512,2]{0,1:T(2,128)S(1)}, f32[512,2,128]{0,2,1:T(8,128)S(1)}) fusion(bf16[2,128,2048]{2,1,0:T(8,128)(2,1)} %bitcast.35, bf16[512,2048]{1,0:T(8,128)(2,1)S(1)} %copy-done), kind=kOutput, calls=%fused_computation.7 | convolution fusion | flops 537132032 | bytes 3674112 | tf_op jit(solution)/shard_map/dot_general | solution.py:37
  40.5 1.0 copy.246
  41.5 6.5 %all-to-all-start.1 = ((bf16[8,256,256]{1,2,0:T(8,128)(2,1)}), bf16[8,256,256]{1,2,0:T(8,128)(2,1)S(1)}, u32[]{:S(2)}, u32[]{:S(2)}) async-start(bf16[8,256,256]{1,2,0:T(8,128)(2,1)} %bitcast.32), calls=%async_computation.1 | async-start | bytes 2097152 | tf_op jit(solution)/shard_map/all_to_all | solution.py:49
  48.1 0.8 copy.139
  49.6 1.1 copy.237
  50.7 1.9 %copy.130 = f32[1,256,256]{1,2,0:T(8,128)} copy(f32[1,256,256]{2,1,0:T(8,128)} %param.110) | data formatting | bytes 524288 | tf_op args[6]
  52.5 1.8 %copy.137 = f32[1,256,256]{1,2,0:T(8,128)} copy(f32[1,256,256]{2,1,0:T(8,128)} %param.111) | data formatting | bytes 524288 | tf_op args[7]
  54.3 1.8 %copy.238 = f32[1,256,256]{1,2,0:T(8,128)} copy(f32[1,256,256]{2,1,0:T(8,128)} %param.109) | data formatting | bytes 524288 | tf_op args[5]
  56.1 5.2 %all-to-all-done.1 = bf16[8,256,256]{1,2,0:T(8,128)(2,1)S(1)} async-done(((bf16[8,256,256]{1,2,0:T(8,128)(2,1)}), bf16[8,256,256]{1,2,0:T(8,128)(2,1)S(1)}, u32[]{:S(2)}, u32[]{:S(2)}) %all-to-all-start.1) | async-done | bytes 1048608 | tf_op jit(solution)/shard_map/all_to_all | solution.py:49
  61.5 2.1 %subtract_convert_fusion = (bf16[1,256,256]{1,2,0:T(8,128)(2,1)S(1)}, bf16[1,256,256]{1,2,0:T(8,128)(2,1)S(1)}, bf16[1,256,256]{1,2,0:T(8,128)(2,1)S(1)}, f32[1,...) fusion(f32[1,256,256]{1,2,0:T(8,128)S(1)} %copy.237, f32[1,256,256]{1,2,0:T(8,128)} %copy.139, ...), kind=kLoop, calls=%fused_computation.21 | loop fusion | flops 1376256 | bytes 2490368 | tf_op jit(solution)/shard_map/convert_element_type | solution.py:59
  63.6 80.4 %conditional.1 = (bf16[3,256,256]{2,1,0:T(8,128)(2,1)}) conditional(s32[]{:T(128)} %clamp.3, bf16[3,256,256]{1,2,0:T(8,128)(2,1)S(1)} %pad_maximum_fusion, bf16[3,256,256]{1,2,0:T(8,128)(2,1)S(1)} %pad_maximum_fusion, bf16[3,256,256]{1,2,0:T(8,128)(2,1)S(1)} %pad_maximum_fusion, ...), branch_computations={%region_3.4_spmd, %region_4.5_spmd, %region_5.6_spmd, %region_6.7_... | conditional | bytes 2359344 | solution.py:21
  64.0 35.4 %collective-permute-start.84 = (bf16[3,256,256]{2,1,0:T(8,128)(2,1)S(1)}, bf16[3,256,256]{2,1,0:T(8,128)(2,1)}, u32[]{:S(2)}, u32[]{:S(2)}) collective-permute-start(bf16[3,256,256]{2,1,0:T(8,128)(2,1)S(1)} %copy.225), channel_id=1, source_target_pairs={{88,0},{96,8},{104,16},{112,24},{120,32},{128,40},{136,48},{144,56... | collective-permute-start | bytes 1179656 | tf_op jit(solution)/shard_map/cond/branch_84_fun/ppermute | solution.py:13
  99.4 44.6 %collective-permute-done.84 = bf16[3,256,256]{2,1,0:T(8,128)(2,1)} collective-permute-done((bf16[3,256,256]{2,1,0:T(8,128)(2,1)S(1)}, bf16[3,256,256]{2,1,0:T(8,128)(2,1)}, u32[]{:S(2)}, u32[]{:S(2)}) %collective-permute-start.84) | collective-permute-done | bytes 393248 | tf_op jit(solution)/shard_map/cond/branch_84_fun/ppermute | solution.py:13
  144.0 1.2 copy.236
  145.3 1.8 %fusion.6 = (f32[1,256,256]{1,2,0:T(8,128)}, f32[1,256,256]{1,2,0:T(8,128)S(1)}) fusion(f32[1,256,256]{1,2,0:T(8,128)S(1)} %copy-done.2, f32[3,256,256]{1,2,0:T(8,128)S(1)} %convert_element_type.54, f32[1,256,256]{1,2,0:T(8,128)} %get-tuple-element.212, f32[1,256,256]{1,2,0:T(8,128)} %copy.238), kind=kLoop, calls=%fused_computation.16 | loop fusion | flops 720896 | bytes 2097152 | tf_op jit(solution)/shard_map/sub | solution.py:66
  147.1 1.8 %copy.239 = f32[1,256,256]{2,1,0:T(8,128)} copy(f32[1,256,256]{1,2,0:T(8,128)} %get-tuple-element.203) | data formatting | bytes 524288
  148.9 0.8 copy.240
  149.8 0.8 copy.241
  (24 shorter events, 2.5 us)
Async XLA Ops:
  0.6 36.8 %copy-start = (bf16[512,2048]{1,0:T(8,128)(2,1)S(1)}, bf16[512,2048]{1,0:T(8,128)(2,1)}, u32[]{:S(2)}) copy-start(bf16[512,2048]{1,0:T(8,128)(2,1)} %param.104) | copy-start | bytes 6291460
  0.6 11.6 %copy-start.4 = (bf16[512,256]{1,0:T(8,128)(2,1)S(1)}, bf16[512,256]{1,0:T(8,128)(2,1)}, u32[]{:S(2)}) copy-start(bf16[512,256]{1,0:T(8,128)(2,1)} %param.105) | copy-start | bytes 786436
  2.9 30.0 %all-to-all-start = ((bf16[8,256,256]{1,2,0:T(8,128)(2,1)}), bf16[8,256,256]{1,2,0:T(8,128)(2,1)}, u32[]{:S(2)}, u32[]{:S(2)}) async-start(bf16[8,256,256]{1,2,0:T(8,128)(2,1)} %broadcast_in_dim.5), calls=%async_computation | async-start | bytes 2097152 | tf_op jit(solution)/shard_map/all_to_all | solution.py:36
  37.4 2.0 %copy-start.5 = (f32[1,128]{1,0:T(1,128)S(1)}, f32[1,128]{1,0:T(1,128)}, u32[]{:S(2)}) copy-start(f32[1,128]{1,0:T(1,128)} %param.106) | copy-start | bytes 1540
  40.5 7.6 %copy-start.3 = (f32[1,256,256]{2,1,0:T(8,128)S(1)}, f32[1,256,256]{2,1,0:T(8,128)}, u32[]{:S(2)}) copy-start(f32[1,256,256]{2,1,0:T(8,128)} %param.107) | copy-start | bytes 786436
  41.5 19.8 %all-to-all-start.1 = ((bf16[8,256,256]{1,2,0:T(8,128)(2,1)}), bf16[8,256,256]{1,2,0:T(8,128)(2,1)S(1)}, u32[]{:S(2)}, u32[]{:S(2)}) async-start(bf16[8,256,256]{1,2,0:T(8,128)(2,1)} %bitcast.32), calls=%async_computation.1 | async-start | bytes 2097152 | tf_op jit(solution)/shard_map/all_to_all | solution.py:49
  50.6 12.9 %copy-start.1 = (f32[1,256,256]{1,2,0:T(8,128)}, f32[1,256,256]{1,2,0:T(8,128)S(1)}, u32[]{:S(2)}) copy-start(f32[1,256,256]{1,2,0:T(8,128)S(1)} %copy.237) | copy-start | bytes 786436
  64.0 80.0 %collective-permute-start.84 = (bf16[3,256,256]{2,1,0:T(8,128)(2,1)S(1)}, bf16[3,256,256]{2,1,0:T(8,128)(2,1)}, u32[]{:S(2)}, u32[]{:S(2)}) collective-permute-start(bf16[3,256,256]{2,1,0:T(8,128)(2,1)S(1)} %copy.225), channel_id=1, source_target_pairs={{88,0},{96,8},{104,16},{112,24},{120,32},{128,40},{136,48},{144,56... | collective-permute-start | bytes 1179656 | tf_op jit(solution)/shard_map/cond/branch_84_fun/ppermute | solution.py:13
  144.0 1.3 copy-start.2
where the time goes:
time: 152 us; the launch traced here: 151 us
  waiting for transfers between devices  70.4 us (46%)
  starting transfers between devices  51.2 us (34%)
  local copies, waits for them, and re-layouts  19.9 us (13%)
  other arithmetic  5.56 us (4%)
  matrix products  2.71 us (2%)
    ppermute x1, waiting for transfers between devices, from_behind(): return lax.ppermute(block, axis, route)  44.6 us
    ppermute x1, starting transfers between devices, from_behind(): return lax.ppermute(block, axis, route)  35.4 us
    all_to_all x1, waiting for transfers between devices, local(): lax.all_to_all(w_copies, 'fsdp', 0, 0, tiled=True)  20.5 us
    unnamed x21, local copies, waits for them, and re-layouts  11.7 us
    all_to_all x1, starting transfers between devices, local(): lax.all_to_all(w_copies, 'fsdp', 0, 0, tiled=True)  9.28 us
    all_to_all x1, starting transfers between devices, local(): lax.all_to_all(grad_terms.astype(jnp.bfloat16), 'fsdp', 0, 0, tiled=True)  6.53 us
    all_to_all x1, waiting for transfers between devices, local(): lax.all_to_all(grad_terms.astype(jnp.bfloat16), 'fsdp', 0, 0, tiled=True)  5.25 us
  transfers between devices with their start and end apart: 3, of which 3 were waited for; matrix products, arithmetic and copies ran while one was open for 5% of the time, Pallas kernels for 0%

commit v1 on v0

--- a/solution.py
+++ b/solution.py
@@ -1,6 +1,7 @@
 import jax
 import jax.numpy as jnp
 from jax import lax
+from jax.experimental.layout import Layout, with_layout_constraint
 from jax.sharding import PartitionSpec as P
 
 HEAD = 128
@@ -33,21 +34,23 @@
     columns = tokens
     count_fsdp = lax.axis_size("fsdp")
     w_copies = jnp.broadcast_to(w_bf[None], (count_fsdp,) + w_bf.shape)
-    w_full = lax.all_to_all(w_copies, "fsdp", 0, 0, tiled=True).reshape(-1, w_bf.shape[1])
-    keys = jnp.dot(columns, w_full, preferred_element_type=jnp.float32)
+    w_pieces = lax.all_to_all(w_copies, "fsdp", 0, 0, tiled=True)
+    columns = tokens.reshape(count_tok, count_fsdp, -1)
+    keys = lax.dot_general(
+        columns, w_pieces, (((1, 2), (0, 1)), ((), ())), preferred_element_type=jnp.float32
+    )
     heads = keys.reshape(count_tok, -1, HEAD)
     scale = lax.rsqrt(jnp.mean(heads * heads, axis=-1, keepdims=True) + 1e-06)
     unit = heads * scale
     g_out = out_grad.astype(jnp.float32).reshape(heads.shape) * gain[0]
     inner_prod = jnp.mean(unit * g_out, axis=-1, keepdims=True)
     key_grad = (scale * (g_out - unit * inner_prod)).reshape(keys.shape).astype(jnp.bfloat16)
-    columns = tokens
     grad_terms = lax.dot_general(
         columns, key_grad, (((0,), (0,)), ((), ())), preferred_element_type=jnp.float32
     )
-    grad_terms = grad_terms.reshape((count_fsdp, -1) + grad_terms.shape[1:])
     grad_parts = lax.all_to_all(grad_terms.astype(jnp.bfloat16), "fsdp", 0, 0, tiled=True)
     grad = grad_parts.astype(jnp.float32).sum(axis=0)
+    grad = with_layout_constraint(grad, Layout((0, 1)))
     first_new = 0.9 * adam_m[0] + 0.1 * grad
     second_new = 0.95 * adam_v[0] + 0.05 * grad * grad
     fix_one = 1.0 - 0.9**ADAM_STEP

time: 152 us -> 97 us (0.64)
  the two profiles are of different devices: /device:TPU:65 before, /device:TPU:22 now
where the time goes in v1:
time: 97 us; the launch traced here: 96.7 us
  waiting for transfers between devices  53.9 us (56%)
  starting transfers between devices  30 us (31%)
  other arithmetic  4.45 us (5%)
  matrix products  4.09 us (4%)
  local copies, waits for them, and re-layouts  2.71 us (3%)
  between operations  1.45 us (1%)
    all_to_all x1, waiting for transfers between devices, local(): w_pieces = lax.all_to_all(w_copies, 'fsdp', 0, 0, tiled=True)  28 us
    all_to_all x1, waiting for transfers between devices, local(): lax.all_to_all(grad_terms.astype(jnp.bfloat16), 'fsdp', 0, 0, tiled=True)  20.6 us
    ppermute x1, starting transfers between devices, from_behind(): return lax.ppermute(block, axis, route)  16.8 us
    all_to_all x1, starting transfers between devices, local(): w_pieces = lax.all_to_all(w_copies, 'fsdp', 0, 0, tiled=True)  8.24 us
    ppermute x1, waiting for transfers between devices, from_behind(): return lax.ppermute(block, axis, route)  5.27 us
    all_to_all x1, starting transfers between devices, local(): lax.all_to_all(grad_terms.astype(jnp.bfloat16), 'fsdp', 0, 0, tiled=True)  5.02 us
    dot_general x1, matrix products, local(): lax.dot_general(columns, w_pieces, (((1, 2), (0, 1)), ((), ())), preferre...  2.36 us
  transfers between devices with their start and end apart: 3, of which 3 were waited for; matrix products, arithmetic and copies ran while one was open for 0% of the time, Pallas kernels for 0%

profile of v1, /device:TPU:22, one launch (start us, length us, event | category | flops | bytes accessed | tf_op | source)
XLA Modules:
  0.0 96.7 jit_solution(13808710300840323917)
XLA Ops:
  0.6 1.0 %convert_bitcast_fusion.1 = bf16[256,256]{1,0:T(8,128)(2,1)S(1)} fusion(f32[1,256,256]{2,1,0:T(8,128)} %param.107), kind=kLoop, calls=%fused_computation.35 | loop fusion | flops 65536 | bytes 393216 | tf_op jit(solution)/shard_map/broadcast_in_dim | solution.py:36
  1.7 0.1 copy.21
  1.8 1.0 %broadcast_in_dim.23 = bf16[8,256,256]{1,2,0:T(8,128)(2,1)} broadcast(bf16[256,256]{0,1:T(8,128)(2,1)S(1)} %copy.21), dimensions={1,2} | broadcast | bytes 1179648 | tf_op jit(solution)/shard_map/broadcast_in_dim | solution.py:36
  2.8 8.2 %all-to-all-start = ((bf16[8,256,256]{1,2,0:T(8,128)(2,1)}), bf16[8,256,256]{1,2,0:T(8,128)(2,1)S(1)}, u32[]{:S(2)}, u32[]{:S(2)}) async-start(bf16[8,256,256]{1,2,0:T(8,128)(2,1)} %broadcast_in_dim.23), calls=%async_computation | async-start | bytes 2097152 | tf_op jit(solution)/shard_map/all_to_all | solution.py:37
  11.0 0.1 copy.25
  11.2 28.0 %all-to-all-done = bf16[8,256,256]{1,2,0:T(8,128)(2,1)S(1)} async-done(((bf16[8,256,256]{1,2,0:T(8,128)(2,1)}), bf16[8,256,256]{1,2,0:T(8,128)(2,1)S(1)}, u32[]{:S(2)}, u32[]{:S(2)}) %all-to-all-start) | async-done | bytes 1048608 | tf_op jit(solution)/shard_map/all_to_all | solution.py:37
  39.2 2.4 %multiply_reduce_fusion.1 = (f32[512,2]{0,1:T(2,128)S(1)}, f32[512,2,128]{0,2,1:T(8,128)S(1)}) fusion(bf16[2,128,8,256]{3,1,0,2:T(8,128)(2,1)S(1)} %bitcast.112, bf16[64,8,8,256]{3,2,1,0:T(8,128)(2,1)} %bitcast.116), kind=kOutput, calls=%fused_computation.12 | convolution fusion | flops 537132032 | bytes 3674112 | tf_op jit(solution)/shard_map/dot_general | solution.py:39
  41.6 0.0 copy-start.7
  41.6 0.1 multiply_reduce_fusion
  41.8 0.1 multiply_convert_fusion
  41.9 1.3 %copy-done.7 = bf16[512,2048]{1,0:T(8,128)(2,1)S(1)} copy-done((bf16[512,2048]{1,0:T(8,128)(2,1)S(1)}, bf16[512,2048]{1,0:T(8,128)(2,1)}, u32[]{:S(2)}) %copy-start.7) | copy-done | bytes 2097176
  43.2 1.7 %fusion.8 = bf16[8,256,256]{1,2,0:T(8,128)(2,1)} fusion(bf16[512,256,1]{0,1,2:T(8,128)(2,1)S(1)} %bitcast.113, bf16[64,8,8,256]{3,2,1,0:T(8,128)(2,1)S(1)} %bitcast.117), kind=kOutput, calls=%fused_computation.8 | convolution fusion | flops 537395200 | bytes 3407872 | tf_op jit(solution)/shard_map/dot_general | solution.py:48
  44.9 5.0 %all-to-all-start.1 = ((bf16[8,256,256]{1,2,0:T(8,128)(2,1)}), bf16[8,256,256]{1,2,0:T(8,128)(2,1)S(1)}, u32[]{:S(2)}, u32[]{:S(2)}) async-start(bf16[8,256,256]{1,2,0:T(8,128)(2,1)} %fusion.8), calls=%async_computation.1 | async-start | bytes 2097152 | tf_op jit(solution)/shard_map/all_to_all | solution.py:51
  50.6 0.0 copy-done
  50.6 20.6 %all-to-all-done.1 = bf16[8,256,256]{1,2,0:T(8,128)(2,1)S(1)} async-done(((bf16[8,256,256]{1,2,0:T(8,128)(2,1)}), bf16[8,256,256]{1,2,0:T(8,128)(2,1)S(1)}, u32[]{:S(2)}, u32[]{:S(2)}) %all-to-all-start.1) | async-done | bytes 1048608 | tf_op jit(solution)/shard_map/all_to_all | solution.py:51
  71.2 0.1 convert_reduce_fusion
  71.4 0.1 copy.27
  71.5 0.0 copy-start.5
  71.5 1.0 %convert_bitcast_fusion = (bf16[1,256,256]{2,1,0:T(8,128)(2,1)S(1)}, f32[256,256]{1,0:T(8,128)S(1)}, f32[1,256,256]{2,1,0:T(8,128)}, f32[1,256,256]{2,1,0:T(8,128)}) fusion(f32[256,256]{1,0:T(8,128)S(1)} %copy.27, f32[1,256,256]{2,1,0:T(8,128)S(1)} %copy-done.3, f32[1,256,256]{2,1,0:T(8,128)S(1)} %copy-done.4, f32[1,256,256]{2,1,0:T(8,128)S(1)} %copy-done.1, ...), kind=kLoop, calls=%fused_computation.34 | loop fusion | flops 1114112 | bytes 2228224 | tf_op jit(solution)/shard_map/stack | solution.py:63
  72.6 22.1 %conditional.1 = (bf16[3,256,256]{2,1,0:T(8,128)(2,1)}) conditional(s32[]{:T(128)} %clamp.3, bf16[3,256,256]{2,1,0:T(8,128)(2,1)S(1)} %pad_maximum_fusion, bf16[3,256,256]{2,1,0:T(8,128)(2,1)S(1)} %pad_maximum_fusion, bf16[3,256,256]{2,1,0:T(8,128)(2,1)S(1)} %pad_maximum_fusion, ...), branch_computations={%region_3.4_spmd, %region_4.5_spmd, %region_5.6_spmd, %region_6.7_... | conditional | bytes 1572912 | solution.py:22
  72.6 16.8 %collective-permute-start.22 = (bf16[3,256,256]{2,1,0:T(8,128)(2,1)S(1)}, bf16[3,256,256]{2,1,0:T(8,128)(2,1)}, u32[]{:S(2)}, u32[]{:S(2)}) collective-permute-start(bf16[3,256,256]{2,1,0:T(8,128)(2,1)S(1)} %param.22), channel_id=1, source_target_pairs={{584,0},{592,8},{600,16},{608,24},{616,32},{624,40},{632,48},{640,... | collective-permute-start | bytes 1179656 | tf_op jit(solution)/shard_map/cond/branch_22_fun/ppermute | solution.py:14
  89.4 5.3 %collective-permute-done.22 = bf16[3,256,256]{2,1,0:T(8,128)(2,1)} collective-permute-done((bf16[3,256,256]{2,1,0:T(8,128)(2,1)S(1)}, bf16[3,256,256]{2,1,0:T(8,128)(2,1)}, u32[]{:S(2)}, u32[]{:S(2)}) %collective-permute-start.22) | collective-permute-done | bytes 393248 | tf_op jit(solution)/shard_map/cond/branch_22_fun/ppermute | solution.py:14
  94.7 1.1 %convert_element_type.49 = f32[3,256,256]{2,1,0:T(8,128)S(1)} convert(bf16[3,256,256]{2,1,0:T(8,128)(2,1)} %get-tuple-element.205) | non-fusion elementwise | flops 196608 | bytes 1179648 | tf_op jit(solution)/shard_map/convert_element_type | solution.py:64
  95.8 0.9 fusion.23
  (16 shorter events, 0.1 us)
Async XLA Ops:
  0.6 10.4 %copy-start.2 = (bf16[512,256]{1,0:T(8,128)(2,1)S(1)}, bf16[512,256]{1,0:T(8,128)(2,1)}, u32[]{:S(2)}) copy-start(bf16[512,256]{1,0:T(8,128)(2,1)} %param.105) | copy-start | bytes 786436
  2.8 36.4 %all-to-all-start = ((bf16[8,256,256]{1,2,0:T(8,128)(2,1)}), bf16[8,256,256]{1,2,0:T(8,128)(2,1)S(1)}, u32[]{:S(2)}, u32[]{:S(2)}) async-start(bf16[8,256,256]{1,2,0:T(8,128)(2,1)} %broadcast_in_dim.23), calls=%async_computation | async-start | bytes 2097152 | tf_op jit(solution)/shard_map/all_to_all | solution.py:37
  39.2 2.4 %copy-start.6 = (f32[1,128]{1,0:T(1,128)S(1)}, f32[1,128]{1,0:T(1,128)}, u32[]{:S(2)}) copy-start(f32[1,128]{1,0:T(1,128)} %param.106) | copy-start | bytes 1540
  41.6 1.6 %copy-start.7 = (bf16[512,2048]{1,0:T(8,128)(2,1)S(1)}, bf16[512,2048]{1,0:T(8,128)(2,1)}, u32[]{:S(2)}) copy-start(bf16[512,2048]{1,0:T(8,128)(2,1)} %param.104) | copy-start | bytes 6291460
  43.2 7.4 %copy-start = (f32[1,256,256]{2,1,0:T(8,128)S(1)}, f32[1,256,256]{2,1,0:T(8,128)}, u32[]{:S(2)}) copy-start(f32[1,256,256]{2,1,0:T(8,128)} %param.108) | copy-start | bytes 786436
  44.9 26.6 %copy-start.1 = (f32[1,256,256]{2,1,0:T(8,128)S(1)}, f32[1,256,256]{2,1,0:T(8,128)}, u32[]{:S(2)}) copy-start(f32[1,256,256]{2,1,0:T(8,128)} %param.107) | copy-start | bytes 786436
  44.9 26.6 %copy-start.3 = (f32[1,256,256]{2,1,0:T(8,128)S(1)}, f32[1,256,256]{2,1,0:T(8,128)}, u32[]{:S(2)}) copy-start(f32[1,256,256]{2,1,0:T(8,128)} %param.111) | copy-start | bytes 786436
  44.9 26.6 %copy-start.4 = (f32[1,256,256]{2,1,0:T(8,128)S(1)}, f32[1,256,256]{2,1,0:T(8,128)}, u32[]{:S(2)}) copy-start(f32[1,256,256]{2,1,0:T(8,128)} %param.110) | copy-start | bytes 786436
  44.9 26.3 %all-to-all-start.1 = ((bf16[8,256,256]{1,2,0:T(8,128)(2,1)}), bf16[8,256,256]{1,2,0:T(8,128)(2,1)S(1)}, u32[]{:S(2)}, u32[]{:S(2)}) async-start(bf16[8,256,256]{1,2,0:T(8,128)(2,1)} %fusion.8), calls=%async_computation.1 | async-start | bytes 2097152 | tf_op jit(solution)/shard_map/all_to_all | solution.py:51
  71.5 24.2 %copy-start.5 = (f32[1,256,256]{2,1,0:T(8,128)S(1)}, f32[1,256,256]{2,1,0:T(8,128)}, u32[]{:S(2)}) copy-start(f32[1,256,256]{2,1,0:T(8,128)} %param.109) | copy-start | bytes 786436
  72.6 22.1 %collective-permute-start.22 = (bf16[3,256,256]{2,1,0:T(8,128)(2,1)S(1)}, bf16[3,256,256]{2,1,0:T(8,128)(2,1)}, u32[]{:S(2)}, u32[]{:S(2)}) collective-permute-start(bf16[3,256,256]{2,1,0:T(8,128)(2,1)S(1)} %param.22), channel_id=1, source_target_pairs={{584,0},{592,8},{600,16},{608,24},{616,32},{624,40},{632,48},{640,... | collective-permute-start | bytes 1179656 | tf_op jit(solution)/shard_map/cond/branch_22_fun/ppermute | solution.py:14
